TPU v7x, 512 devices: a whole 4x4x16 slice. The times are simulated.
512 devices in a mesh: row: 32 (over z, y_lo), col: 16 (over x, y_hi, core).
Axes of the slice: x: 4, y: 4 (y_hi: 2, y_lo: 2; y = y_hi * 2 + y_lo), z: 16, core: 2. Of those that a mesh axis runs over, the one named last changes fastest.
Arguments:
- inputs: bfloat16 [1, 256, 256, 1024], P(None, 'row', 'col'), may hold values from -6 to 6
- norm_gain: float32 [1024], replicated, may hold values from 0.1 to 1.9
- w_query: bfloat16 [1024, 512], P('row'), may hold values from -8 to 8
- w_keyvalue: bfloat16 [1024, 1024], P('row'), may hold values from -0.1875 to 0.1875
- w_output: bfloat16 [512, 1024], P('row'), may hold values from -0.25 to 0.25
- out_grad: bfloat16 [1, 256, 256, 1024], P(None, 'row', 'col'), may hold values from -6 to 6
Outputs:
- layer_out: bfloat16 [1, 256, 256, 1024], P(None, 'row', 'col')
- in_grad: bfloat16 [1, 256, 256, 1024], P(None, 'row', 'col')
- keyvalue_grad: float32 [1024, 1024], P('row')
All inputs are finite; a program needn't handle non-finite values.
Results may differ from a plain program's by a relative error of at most 0.012.
The roundings to bfloat16 on the way count: a program that leaves them out, or rounds other values in their place, can miss the bound.
Values may be sent and summed in bfloat16 or wider, within the bound.
No kernel may reach another device: no remote copies, remote signals or barrier semaphores. Data moves between devices by JAX's collectives and lax.ppermute only.
A program may use at most 64 MiB of HBM per device.

v0:
```python
import math
import jax
import jax.numpy as jnp
from jax import lax
from jax.sharding import PartitionSpec as P

HEADS = 8
RADIUS = 6
EPS = 1e-05
MASKED = -1e30


def shifted(value, axis, steps):
    count = lax.axis_size(axis)
    first, last = (max(0, -steps), min(count, count - steps))
    return lax.ppermute(value, axis, [(source, source + steps) for source in range(first, last)])


def with_halo(block, sides, width):
    for axis, dim in sides:
        count = lax.axis_size(axis)
        forward = [(i, i + 1) for i in range(count - 1)]
        backward = [(target, source) for source, target in forward]
        low = lax.ppermute(
            lax.slice_in_dim(block, block.shape[dim] - width, None, axis=dim), axis, forward
        )
        high = lax.ppermute(lax.slice_in_dim(block, 0, width, axis=dim), axis, backward)
        block = jnp.concatenate([low, block, high], axis=dim)
    return block


def normalize(inputs, norm_gain):
    values = inputs.astype(jnp.float32)
    center = values - jnp.mean(values, axis=-1, keepdims=True)
    spread = lax.rsqrt(jnp.mean(center * center, axis=-1, keepdims=True) + EPS)
    standard = center * spread
    return (standard, spread, (standard * norm_gain).astype(jnp.bfloat16))


def window_mask(row_start, col_start, tile_rows, tile_cols, height, map_width):
    ext_rows = tile_rows + 2 * RADIUS
    ext_cols = tile_cols + 2 * RADIUS
    query_pos = jnp.arange(tile_rows * tile_cols, dtype=jnp.int32)
    query_row = query_pos // tile_cols
    query_col = query_pos % tile_cols
    ext_pos = jnp.arange(ext_rows * ext_cols, dtype=jnp.int32)
    ext_row = ext_pos // ext_cols
    ext_col = ext_pos % ext_cols
    nearby = (jnp.abs(ext_row[None, :] - RADIUS - query_row[:, None]) <= RADIUS) & (
        jnp.abs(ext_col[None, :] - RADIUS - query_col[:, None]) <= RADIUS
    )
    global_row = row_start + ext_row - RADIUS
    global_col = col_start + ext_col - RADIUS
    inside = (
        (global_row >= 0) & (global_row < height) & (global_col >= 0) & (global_col < map_width)
    )
    return nearby & inside[None, :]


def tile_forward(queries, keyvalue_ext, allowed):
    batches, query_count, inner_width = queries.shape
    head_size = inner_width // HEADS
    query_heads = queries.reshape(batches, query_count, HEADS, head_size)
    key_heads = keyvalue_ext[:, :, :inner_width].reshape(batches, -1, HEADS, head_size)
    value_heads = keyvalue_ext[:, :, inner_width:].reshape(batches, -1, HEADS, head_size)
    scores = jnp.einsum(
        "bqhd,bkhd->bhqk", query_heads, key_heads, preferred_element_type=jnp.float32
    ) / math.sqrt(head_size)
    scores = jnp.where(allowed, scores, MASKED)
    row_max = jnp.max(scores, axis=-1, keepdims=True)
    exponent = jnp.exp(scores - row_max)
    soft = exponent / jnp.sum(exponent, axis=-1, keepdims=True)
    rounded = soft.astype(jnp.bfloat16)
    attended = jnp.einsum(
        "bhqk,bkhd->bqhd", rounded, value_heads, preferred_element_type=jnp.float32
    )
    return (attended.astype(jnp.bfloat16).reshape(batches, query_count, inner_width), soft, rounded)


def tile_backward(queries, keyvalue_ext, soft, rounded, inner_grad):
    batches, query_count, inner_width = queries.shape
    head_size = inner_width // HEADS
    query_heads = queries.reshape(batches, query_count, HEADS, head_size)
    key_heads = keyvalue_ext[:, :, :inner_width].reshape(batches, -1, HEADS, head_size)
    value_heads = keyvalue_ext[:, :, inner_width:].reshape(batches, -1, HEADS, head_size)
    grad_heads = inner_grad.reshape(batches, query_count, HEADS, head_size)
    prob_grad = jnp.einsum(
        "bqhd,bkhd->bhqk", grad_heads, value_heads, preferred_element_type=jnp.float32
    )
    row_dot = jnp.sum(soft * prob_grad, axis=-1, keepdims=True)
    score_grad = (soft * (prob_grad - row_dot) / math.sqrt(head_size)).astype(jnp.bfloat16)
    query_grad = jnp.einsum(
        "bhqk,bkhd->bqhd", score_grad, key_heads, preferred_element_type=jnp.float32
    )
    key_grad = jnp.einsum(
        "bhqk,bqhd->bkhd", score_grad, query_heads, preferred_element_type=jnp.float32
    )
    value_grad = jnp.einsum(
        "bhqk,bqhd->bkhd", rounded, grad_heads, preferred_element_type=jnp.float32
    )
    ext_count = key_grad.shape[1]
    joined = jnp.concatenate(
        [
            key_grad.reshape(batches, ext_count, inner_width),
            value_grad.reshape(batches, ext_count, inner_width),
        ],
        axis=-1,
    )
    return (query_grad.astype(jnp.bfloat16).reshape(batches, query_count, inner_width), joined)


def fold_cols(extended):
    left_strip = extended[:, :, :RADIUS]
    right_strip = extended[:, :, extended.shape[2] - RADIUS :]
    middle = extended[:, :, RADIUS : extended.shape[2] - RADIUS]
    from_right = shifted(left_strip, "col", -1)
    from_left = shifted(right_strip, "col", 1)
    inner_cols = middle.shape[2]
    return (
        middle
        + jnp.pad(from_left, ((0, 0), (0, 0), (0, inner_cols - RADIUS), (0, 0)))
        + jnp.pad(from_right, ((0, 0), (0, 0), (inner_cols - RADIUS, 0), (0, 0)))
    )


def fold_rows(extended):
    upper_strip = extended[:, :RADIUS]
    lower_strip = extended[:, extended.shape[1] - RADIUS :]
    middle = extended[:, RADIUS : extended.shape[1] - RADIUS]
    from_below = shifted(upper_strip, "row", -1)
    from_above = shifted(lower_strip, "row", 1)
    inner_rows = middle.shape[1]
    return (
        middle
        + jnp.pad(from_above, ((0, 0), (0, inner_rows - RADIUS), (0, 0), (0, 0)))
        + jnp.pad(from_below, ((0, 0), (inner_rows - RADIUS, 0), (0, 0), (0, 0)))
    )


def local(inputs, norm_gain, w_query, w_keyvalue, w_output, out_grad):
    batches, tile_rows, tile_cols, model_width = inputs.shape
    ext_rows = tile_rows + 2 * RADIUS
    ext_cols = tile_cols + 2 * RADIUS
    standard, spread, normed = normalize(inputs, norm_gain)
    flat_norm = normed.reshape(-1, model_width)
    full_query, full_keyvalue, full_output = (
        lax.all_gather(w_query, "row", axis=0, tiled=True),
        lax.all_gather(w_keyvalue, "row", axis=0, tiled=True),
        lax.all_gather(w_output, "row", axis=0, tiled=True),
    )
    inner_width = full_query.shape[1]
    queries = jnp.dot(flat_norm, full_query, preferred_element_type=jnp.float32).astype(
        jnp.bfloat16
    )
    queries = queries.reshape(batches, tile_rows * tile_cols, inner_width)
    keyvalue = jnp.dot(flat_norm, full_keyvalue, preferred_element_type=jnp.float32).astype(
        jnp.bfloat16
    )
    keyvalue = keyvalue.reshape(batches, tile_rows, tile_cols, 2 * inner_width)
    keyvalue_ext = with_halo(keyvalue, (("row", 1), ("col", 2)), RADIUS)
    keyvalue_ext = keyvalue_ext.reshape(batches, ext_rows * ext_cols, 2 * inner_width)
    allowed = window_mask(
        lax.axis_index("row") * tile_rows,
        lax.axis_index("col") * tile_cols,
        tile_rows,
        tile_cols,
        tile_rows * lax.axis_size("row"),
        tile_cols * lax.axis_size("col"),
    )
    attended, soft, rounded = tile_forward(queries, keyvalue_ext, allowed)
    projected = jnp.dot(
        attended.reshape(-1, inner_width), full_output, preferred_element_type=jnp.float32
    )
    layer_out = (inputs.astype(jnp.float32) + projected.reshape(inputs.shape)).astype(jnp.bfloat16)
    flat_grad = out_grad.reshape(-1, model_width)
    inner_grad = lax.dot_general(
        flat_grad, full_output, (((1,), (1,)), ((), ())), preferred_element_type=jnp.float32
    ).astype(jnp.bfloat16)
    inner_grad = inner_grad.reshape(batches, tile_rows * tile_cols, inner_width)
    query_grad, keyvalue_part = tile_backward(queries, keyvalue_ext, soft, rounded, inner_grad)
    keyvalue_part = keyvalue_part.reshape(batches, ext_rows, ext_cols, 2 * inner_width)
    owned = fold_rows(fold_cols(keyvalue_part))
    token_grad = owned.astype(jnp.bfloat16).reshape(-1, 2 * inner_width)
    rows_part = lax.psum_scatter(
        lax.dot_general(
            flat_norm, token_grad, (((0,), (0,)), ((), ())), preferred_element_type=jnp.float32
        ),
        "row",
        scatter_dimension=0,
        tiled=True,
    )
    keyvalue_grad = lax.psum(rows_part, "col")
    normed_grad = lax.dot_general(
        query_grad.reshape(-1, inner_width),
        full_query,
        (((1,), (1,)), ((), ())),
        preferred_element_type=jnp.float32,
    )
    normed_grad = normed_grad + lax.dot_general(
        token_grad, full_keyvalue, (((1,), (1,)), ((), ())), preferred_element_type=jnp.float32
    )
    gained = normed_grad.reshape(inputs.shape) * norm_gain
    in_grad = out_grad.astype(jnp.float32) + spread * (
        gained
        - jnp.mean(gained, axis=-1, keepdims=True)
        - standard * jnp.mean(gained * standard, axis=-1, keepdims=True)
    )
    return (layer_out, in_grad.astype(jnp.bfloat16), keyvalue_grad)


def solution(mesh):
    return jax.shard_map(
        local,
        mesh=mesh,
        in_specs=(
            P(None, "row", "col", None),
            P(),
            P("row", None),
            P("row", None),
            P("row", None),
            P(None, "row", "col", None),
        ),
        out_specs=(P(None, "row", "col", None), P(None, "row", "col", None), P("row", None)),
        check_vma=False,
    )
```

profile of v0, /device:TPU:1, one launch (start us, length us, event | category | flops | bytes accessed | tf_op | source)
XLA Modules:
  0.0 792.2 jit_solution(14434119171756185005)
XLA Ops:
  13.3 115.3 %all-gather.4.cloned.1.call-done = bf16[1024,1024]{1,0:T(8,128)(2,1)} async-done(((bf16[32,1024]{1,0:T(8,128)(2,1)}), bf16[1024,1024]{1,0:T(8,128)(2,1)}) %all-gather.4.cloned.1.call-update) | async-done | bytes 2097168 | tf_op jit(solution)/shard_map/all_gather | solution.py:148
  128.6 2.0 convolution_convert_fusion
  130.7 2.2 collective-permute-start
  134.2 126.6 %all-gather.8.cloned.1.call-done = bf16[512,1024]{1,0:T(8,128)(2,1)} async-done(((bf16[16,1024]{1,0:T(8,128)(2,1)}), bf16[512,1024]{1,0:T(8,128)(2,1)}) %all-gather.8.cloned.1.call-update) | async-done | bytes 1048592 | tf_op jit(solution)/shard_map/all_gather | solution.py:149
  262.9 26.0 %collective-permute-start.2 = (bf16[1,20,6,1024]{3,2,1,0:T(8,128)(2,1)S(1)}, bf16[1,20,6,1024]{3,2,1,0:T(8,128)(2,1)S(1)}, u32[]{:S(2)}, u32[]{:S(2)}) collective-permute-start(bf16[1,20,6,1024]{3,2,1,0:T(8,128)(2,1)S(1)} %get-tuple-element.9), channel_id=1, source_target_pairs={{0,1},{1,2},{2,3},{3,4},{4,5},{5,6},{6,7},{7,8},{8,9},{9,10},{10,1... | collective-permute-start | bytes 737288 | tf_op jit(solution)/shard_map/ppermute | solution.py:24
  288.8 1.9 collective-permute-start.3
  290.8 102.0 %all-gather.6.cloned.1.call-done = bf16[1024,512]{1,0:T(8,128)(2,1)} async-done(((bf16[32,512]{1,0:T(8,128)(2,1)}), bf16[1024,512]{1,0:T(8,128)(2,1)}) %all-gather.6.cloned.1.call-update) | async-done | bytes 1048592 | tf_op jit(solution)/shard_map/all_gather | solution.py:147
  396.1 2.0 fusion.76
  398.1 2.3 fusion.75
  400.5 2.3 convolution_bitcast_fusion.1
  402.8 2.5 copy.31
  406.8 5.7 fusion.12
  412.4 2.5 copy.30
  415.0 2.4 concatenate.16
  417.4 2.5 constant_dynamic-update-slice_fusion.1
  421.6 26.0 %collective-permute-start.4 = (f32[1,20,6,1024]{3,0,2,1:T(1,128)S(1)}, f32[1,20,6,1024]{3,0,2,1:T(1,128)S(1)}, u32[]{:S(2)}, u32[]{:S(2)}) collective-permute-start(f32[1,20,6,1024]{3,0,2,1:T(1,128)S(1)} %get-tuple-element.3), channel_id=1, source_target_pairs={{0,1},{1,2},{2,3},{3,4},{4,5},{5,6},{6,7},{7,8},{8,9},{9,10},{10,1... | collective-permute-start | bytes 1474568 | tf_op jit(solution)/shard_map/ppermute | solution.py:16
  447.5 2.1 collective-permute-start.5
  449.7 9.1 %collective-permute-done.4 = f32[1,20,6,1024]{3,0,2,1:T(1,128)S(1)} collective-permute-done((f32[1,20,6,1024]{3,0,2,1:T(1,128)S(1)}, f32[1,20,6,1024]{3,0,2,1:T(1,128)S(1)}, u32[]{:S(2)}, u32[]{:S(2)}) %collective-permute-start.4) | collective-permute-done | bytes 491552 | tf_op jit(solution)/shard_map/ppermute | solution.py:16
  463.8 11.6 %collective-permute-done.6 = f32[1,6,16,1024]{3,0,2,1:T(1,128)S(1)} collective-permute-done((f32[1,6,16,1024]{3,0,2,1:T(1,128)S(1)}, f32[1,6,16,1024]{3,0,2,1:T(1,128)S(1)}, u32[]{:S(2)}, u32[]{:S(2)}) %collective-permute-start.6) | collective-permute-done | bytes 393248 | tf_op jit(solution)/shard_map/ppermute | solution.py:16
  476.9 2.7 convolution_bitcast_fusion
  480.6 2.3 fusion.26
  483.4 5.5 fusion.18
  492.7 116.1 %reduce-scatter.2.cloned.1.call-done = f32[32,1024]{1,0:T(8,128)} async-done(((f32[1024,1024]{1,0:T(8,128)}), f32[32,1024]{1,0:T(8,128)}) %reduce-scatter.2.cloned.1.call-update) | async-done | bytes 131088 | tf_op jit(solution)/shard_map/reduce_scatter | solution.py:184
  609.8 174.3 %all-reduce.6.cloned.1.call-done = f32[32,1024]{1,0:T(8,128)} async-done(((f32[32,1024]{1,0:T(8,128)}), f32[32,1024]{1,0:T(8,128)}) %all-reduce.6.cloned.1.call-update) | async-done | bytes 131088 | tf_op jit(solution)/shard_map/psum | solution.py:192
  (90 shorter events, 29.9 us)
Async XLA Ops:
  7.2 121.5 %all-gather.4.cloned.1.call-start = ((), (), s32[]{:S(2)}) async-start(), calls=%async_computation.1 | async-start | bytes 2162688 | tf_op jit(solution)/shard_map/all_gather | solution.py:148
  7.9 252.9 %all-gather.8.cloned.1.call-start = ((), (), s32[]{:S(2)}) async-start(), calls=%async_computation.3 | async-start | bytes 1081344 | tf_op jit(solution)/shard_map/all_gather | solution.py:149
  8.6 384.1 %all-gather.6.cloned.1.call-start = ((), (), s32[]{:S(2)}) async-start(), calls=%async_computation.2 | async-start | bytes 1081344 | tf_op jit(solution)/shard_map/all_gather | solution.py:147
  9.4 599.4 %reduce-scatter.2.cloned.1.call-start = ((), (), s32[]{:S(2)}) async-start(), calls=%async_computation.4 | async-start | bytes 4325376 | tf_op jit(solution)/shard_map/reduce_scatter | solution.py:184
  9.5 251.3 %copy-start.8 = (bf16[1,8,16,1024]{3,2,1,0:T(8,128)(2,1)S(1)}, bf16[1,8,16,1024]{3,2,1,0:T(8,128)(2,1)}, u32[]{:S(2)}) copy-start(bf16[1,8,16,1024]{3,2,1,0:T(8,128)(2,1)} %param.11) | copy-start | bytes 786436
  13.3 379.5 %copy-start.6 = (bf16[1,8,16,1024]{3,2,1,0:T(8,128)(2,1)}, bf16[1,8,16,1024]{3,2,1,0:T(8,128)(2,1)S(1)}, u32[]{:S(2)}) copy-start(bf16[1,8,16,1024]{3,2,1,0:T(8,128)(2,1)S(1)} %fusion.35) | copy-start | bytes 786436
  130.7 131.9 %collective-permute-start = (bf16[1,6,16,1024]{3,2,1,0:T(8,128)(2,1)S(1)}, bf16[1,6,16,1024]{3,2,1,0:T(8,128)(2,1)S(1)}, u32[]{:S(2)}, u32[]{:S(2)}) collective-permute-start(bf16[1,6,16,1024]{3,2,1,0:T(8,128)(2,1)S(1)} %get-tuple-element.11), channel_id=1, source_target_pairs={{0,16},{16,32},{32,48},{48,64},{64,80},{80,96},{96,112},{112,128},... | collective-permute-start | bytes 589832 | tf_op jit(solution)/shard_map/ppermute | solution.py:24
  132.9 129.8 %collective-permute-start.1 = (bf16[1,6,16,1024]{3,2,1,0:T(8,128)(2,1)S(1)}, bf16[1,6,16,1024]{3,2,1,0:T(8,128)(2,1)S(1)}, u32[]{:S(2)}, u32[]{:S(2)}) collective-permute-start(bf16[1,6,16,1024]{3,2,1,0:T(8,128)(2,1)S(1)} %get-tuple-element.12), channel_id=1, source_target_pairs={{16,0},{32,16},{48,32},{64,48},{80,64},{96,80},{112,96},{128,112},... | collective-permute-start | bytes 589832 | tf_op jit(solution)/shard_map/ppermute | solution.py:27
  262.9 131.6 %collective-permute-start.2 = (bf16[1,20,6,1024]{3,2,1,0:T(8,128)(2,1)S(1)}, bf16[1,20,6,1024]{3,2,1,0:T(8,128)(2,1)S(1)}, u32[]{:S(2)}, u32[]{:S(2)}) collective-permute-start(bf16[1,20,6,1024]{3,2,1,0:T(8,128)(2,1)S(1)} %get-tuple-element.9), channel_id=1, source_target_pairs={{0,1},{1,2},{2,3},{3,4},{4,5},{5,6},{6,7},{7,8},{8,9},{9,10},{10,1... | collective-permute-start | bytes 737288 | tf_op jit(solution)/shard_map/ppermute | solution.py:24
  288.8 105.7 %collective-permute-start.3 = (bf16[1,20,6,1024]{3,2,1,0:T(8,128)(2,1)S(1)}, bf16[1,20,6,1024]{3,2,1,0:T(8,128)(2,1)S(1)}, u32[]{:S(2)}, u32[]{:S(2)}) collective-permute-start(bf16[1,20,6,1024]{3,2,1,0:T(8,128)(2,1)S(1)} %get-tuple-element.10), channel_id=1, source_target_pairs={{1,0},{2,1},{3,2},{4,3},{5,4},{6,5},{7,6},{8,7},{9,8},{10,9},{11,1... | collective-permute-start | bytes 737288 | tf_op jit(solution)/shard_map/ppermute | solution.py:27
  394.5 6.0 copy-start.13
  395.8 4.7 copy-start.11
  396.1 4.4 copy-start.4
  421.6 37.2 %collective-permute-start.4 = (f32[1,20,6,1024]{3,0,2,1:T(1,128)S(1)}, f32[1,20,6,1024]{3,0,2,1:T(1,128)S(1)}, u32[]{:S(2)}, u32[]{:S(2)}) collective-permute-start(f32[1,20,6,1024]{3,0,2,1:T(1,128)S(1)} %get-tuple-element.3), channel_id=1, source_target_pairs={{0,1},{1,2},{2,3},{3,4},{4,5},{5,6},{6,7},{7,8},{8,9},{9,10},{10,1... | collective-permute-start | bytes 1474568 | tf_op jit(solution)/shard_map/ppermute | solution.py:16
  447.5 11.7 %collective-permute-start.5 = (f32[1,20,6,1024]{3,0,2,1:T(1,128)S(1)}, f32[1,20,6,1024]{3,0,2,1:T(1,128)S(1)}, u32[]{:S(2)}, u32[]{:S(2)}) collective-permute-start(f32[1,20,6,1024]{3,0,2,1:T(1,128)S(1)} %get-tuple-element.4), channel_id=1, source_target_pairs={{1,0},{2,1},{3,2},{4,3},{5,4},{6,5},{7,6},{8,7},{9,8},{10,9},{11,1... | collective-permute-start | bytes 1474568 | tf_op jit(solution)/shard_map/ppermute | solution.py:16
  460.7 16.2 %copy-start.7 = (bf16[1,8,16,1024]{3,2,1,0:T(8,128)(2,1)S(1)}, bf16[1,8,16,1024]{3,2,1,0:T(8,128)(2,1)}, u32[]{:S(2)}) copy-start(bf16[1,8,16,1024]{3,2,1,0:T(8,128)(2,1)} %copy-done.6) | copy-start | bytes 786436
  461.2 14.2 %collective-permute-start.6 = (f32[1,6,16,1024]{3,0,2,1:T(1,128)S(1)}, f32[1,6,16,1024]{3,0,2,1:T(1,128)S(1)}, u32[]{:S(2)}, u32[]{:S(2)}) collective-permute-start(f32[1,6,16,1024]{3,0,2,1:T(1,128)S(1)} %get-tuple-element.5), channel_id=1, source_target_pairs={{0,16},{16,32},{32,48},{48,64},{64,80},{80,96},{96,112},{112,128},... | collective-permute-start | bytes 1179656 | tf_op jit(solution)/shard_map/ppermute | solution.py:16
  462.5 12.9 %collective-permute-start.7 = (f32[1,6,16,1024]{3,0,2,1:T(1,128)S(1)}, f32[1,6,16,1024]{3,0,2,1:T(1,128)S(1)}, u32[]{:S(2)}, u32[]{:S(2)}) collective-permute-start(f32[1,6,16,1024]{3,0,2,1:T(1,128)S(1)} %get-tuple-element.6), channel_id=1, source_target_pairs={{16,0},{32,16},{48,32},{64,48},{80,64},{96,80},{112,96},{128,112},... | collective-permute-start | bytes 1179656 | tf_op jit(solution)/shard_map/ppermute | solution.py:16
  479.6 304.6 %all-reduce.6.cloned.1.call-start = ((), (), s32[]{:S(2)}) async-start(), calls=%async_computation.5 | async-start | bytes 262144 | tf_op jit(solution)/shard_map/psum | solution.py:192
  483.4 5.6 copy-start
  483.4 5.6 copy-start.3
  483.4 6.6 copy-start.1
  489.0 2.9 copy-start.12
  491.8 117.1 %copy-start.9 = (bf16[1,8,16,1024]{3,2,1,0:T(8,128)(2,1)S(1)}, bf16[1,8,16,1024]{3,2,1,0:T(8,128)(2,1)}, u32[]{:S(2)}) copy-start(bf16[1,8,16,1024]{3,2,1,0:T(8,128)(2,1)} %param.11) | copy-start | bytes 786436
  (5 other events, 8.6 us)
Sparse Core Ops, SparseCore 0:
  10.1 118.4 all-gather.3
  130.7 130.0 all-gather.7
  262.9 129.8 all-gather.5
  479.7 129.0 reduce-scatter.1
  611.5 172.5 all-reduce.5
where the time goes:
time: 793 us; the launch traced here: 792 us
  waiting for transfers between devices  658 us (83%)
  starting transfers between devices  62.2 us (8%)
  matrix products  31.5 us (4%)
  local copies, waits for them, and re-layouts  18.8 us (2%)
  between operations  14.3 us (2%)
    psum x1, waiting for transfers between devices, local(): keyvalue_grad = lax.psum(rows_part, 'col')  174 us
    all_gather x1, waiting for transfers between devices, local(): lax.all_gather(w_output, 'row', axis=0, tiled=True)  127 us
    reduce_scatter x1, waiting for transfers between devices, local(): lax.psum_scatter(lax.dot_general(flat_norm, token_grad, (((0,), (0,)), ((...  116 us
    all_gather x1, waiting for transfers between devices, local(): lax.all_gather(w_keyvalue, 'row', axis=0, tiled=True)  115 us
    all_gather x1, waiting for transfers between devices, local(): lax.all_gather(w_query, 'row', axis=0, tiled=True)  102 us
    ppermute x4, starting transfers between devices, shifted(): lax.ppermute(value, axis, [(source, source + steps) for source in range(f...  30.7 us
    ppermute x2, starting transfers between devices, with_halo(): lax.ppermute(lax.slice_in_dim(block, block.shape[dim] - width, None, axis...  28.1 us
    ppermute x4, waiting for transfers between devices, shifted(): lax.ppermute(value, axis, [(source, source + steps) for source in range(f...  21.1 us
  transfers between devices with their start and end apart: 13, of which 8 were waited for; matrix products, arithmetic and copies ran while one was open for 3% of the time, Pallas kernels for 0%

commit v1 on v0

--- a/solution.py
+++ b/solution.py
@@ -189,7 +189,7 @@
         scatter_dimension=0,
         tiled=True,
     )
-    keyvalue_grad = lax.psum(rows_part, "col")
+    keyvalue_grad = jnp.sum(lax.all_gather(rows_part, "col"), axis=0)
     normed_grad = lax.dot_general(
         query_grad.reshape(-1, inner_width),
         full_query,

time: 793 us -> 706 us (0.89)
  waiting for transfers between devices: 658 us -> 571 us
    psum x1 -> x0, waiting for transfers between devices: 174 us -> none  [local(): keyvalue_grad = lax.psum(rows_part, 'col')]
    all_gather x0 -> x1, waiting for transfers between devices: none -> 75 us  [local(): keyvalue_grad = jnp.sum(lax.all_gather(rows_part, 'col'), axis=0)]
    reduce_scatter x1, waiting for transfers between devices: 116 us -> 129 us  [local(): lax.psum_scatter(lax.dot_general(flat_norm, token_grad, (((0,), (0,)), ((...]
where the time goes in v1:
time: 706 us
  waiting for transfers between devices  571 us (81%)
  starting transfers between devices  62.2 us (9%)
  matrix products  31.5 us (4%)
  local copies, waits for them, and re-layouts  16.2 us (2%)
  between operations  14.3 us (2%)
  other arithmetic  10.2 us (1%)
    reduce_scatter x1, waiting for transfers between devices, local(): lax.psum_scatter(lax.dot_general(flat_norm, token_grad, (((0,), (0,)), ((...  129 us
    all_gather x1, waiting for transfers between devices, local(): lax.all_gather(w_output, 'row', axis=0, tiled=True)  127 us
    all_gather x1, waiting for transfers between devices, local(): lax.all_gather(w_keyvalue, 'row', axis=0, tiled=True)  115 us
    all_gather x1, waiting for transfers between devices, local(): lax.all_gather(w_query, 'row', axis=0, tiled=True)  102 us
    all_gather x1, waiting for transfers between devices, local(): keyvalue_grad = jnp.sum(lax.all_gather(rows_part, 'col'), axis=0)  75 us
    ppermute x4, starting transfers between devices, shifted(): lax.ppermute(value, axis, [(source, source + steps) for source in range(f...  30.7 us
    ppermute x2, starting transfers between devices, with_halo(): lax.ppermute(lax.slice_in_dim(block, block.shape[dim] - width, None, axis...  28.1 us
    ppermute x4, waiting for transfers between devices, shifted(): lax.ppermute(value, axis, [(source, source + steps) for source in range(f...  21.1 us
  transfers between devices with their start and end apart: 13, of which 8 were waited for; matrix products, arithmetic and copies ran while one was open for 3% of the time, Pallas kernels for 0%

profile of v1, /device:TPU:1, one launch (start us, length us, event | category | flops | bytes accessed | tf_op | source)
XLA Modules:
  0.0 705.8 jit_solution(13289561855208643378)
XLA Ops:
  13.3 115.3 %all-gather.6.cloned.1.call-done = bf16[1024,1024]{1,0:T(8,128)(2,1)} async-done(((bf16[32,1024]{1,0:T(8,128)(2,1)}), bf16[1024,1024]{1,0:T(8,128)(2,1)}) %all-gather.6.cloned.1.call-update) | async-done | bytes 2097168 | tf_op jit(solution)/shard_map/all_gather | solution.py:148
  128.6 2.0 convolution_convert_fusion
  130.7 2.2 collective-permute-start
  134.2 126.6 %all-gather.10.cloned.1.call-done = bf16[512,1024]{1,0:T(8,128)(2,1)} async-done(((bf16[16,1024]{1,0:T(8,128)(2,1)}), bf16[512,1024]{1,0:T(8,128)(2,1)}) %all-gather.10.cloned.1.call-update) | async-done | bytes 1048592 | tf_op jit(solution)/shard_map/all_gather | solution.py:149
  262.9 26.0 %collective-permute-start.2 = (bf16[1,20,6,1024]{3,2,1,0:T(8,128)(2,1)S(1)}, bf16[1,20,6,1024]{3,2,1,0:T(8,128)(2,1)S(1)}, u32[]{:S(2)}, u32[]{:S(2)}) collective-permute-start(bf16[1,20,6,1024]{3,2,1,0:T(8,128)(2,1)S(1)} %get-tuple-element.9), channel_id=1, source_target_pairs={{0,1},{1,2},{2,3},{3,4},{4,5},{5,6},{6,7},{7,8},{8,9},{9,10},{10,1... | collective-permute-start | bytes 737288 | tf_op jit(solution)/shard_map/ppermute | solution.py:24
  290.8 102.0 %all-gather.8.cloned.1.call-done = bf16[1024,512]{1,0:T(8,128)(2,1)} async-done(((bf16[32,512]{1,0:T(8,128)(2,1)}), bf16[1024,512]{1,0:T(8,128)(2,1)}) %all-gather.8.cloned.1.call-update) | async-done | bytes 1048592 | tf_op jit(solution)/shard_map/all_gather | solution.py:147
  396.1 2.0 fusion.76
  398.1 2.3 fusion.75
  400.5 2.3 convolution_bitcast_fusion.1
  402.8 2.5 copy.31
  406.8 5.7 fusion.12
  412.4 2.5 copy.30
  415.0 2.4 concatenate.16
  417.4 2.5 constant_dynamic-update-slice_fusion.1
  421.6 26.0 %collective-permute-start.4 = (f32[1,20,6,1024]{3,0,2,1:T(1,128)S(1)}, f32[1,20,6,1024]{3,0,2,1:T(1,128)S(1)}, u32[]{:S(2)}, u32[]{:S(2)}) collective-permute-start(f32[1,20,6,1024]{3,0,2,1:T(1,128)S(1)} %get-tuple-element.3), channel_id=1, source_target_pairs={{0,1},{1,2},{2,3},{3,4},{4,5},{5,6},{6,7},{7,8},{8,9},{9,10},{10,1... | collective-permute-start | bytes 1474568 | tf_op jit(solution)/shard_map/ppermute | solution.py:16
  447.5 2.1 collective-permute-start.5
  449.7 9.1 %collective-permute-done.4 = f32[1,20,6,1024]{3,0,2,1:T(1,128)S(1)} collective-permute-done((f32[1,20,6,1024]{3,0,2,1:T(1,128)S(1)}, f32[1,20,6,1024]{3,0,2,1:T(1,128)S(1)}, u32[]{:S(2)}, u32[]{:S(2)}) %collective-permute-start.4) | collective-permute-done | bytes 491552 | tf_op jit(solution)/shard_map/ppermute | solution.py:16
  463.8 11.6 %collective-permute-done.6 = f32[1,6,16,1024]{3,0,2,1:T(1,128)S(1)} collective-permute-done((f32[1,6,16,1024]{3,0,2,1:T(1,128)S(1)}, f32[1,6,16,1024]{3,0,2,1:T(1,128)S(1)}, u32[]{:S(2)}, u32[]{:S(2)}) %collective-permute-start.6) | collective-permute-done | bytes 393248 | tf_op jit(solution)/shard_map/ppermute | solution.py:16
  476.9 2.7 convolution_bitcast_fusion
  479.6 129.2 %reduce-scatter.2.cloned.1.call-done = f32[32,1024]{1,0:T(8,128)} async-done(((f32[1024,1024]{1,0:T(8,128)}), f32[32,1024]{1,0:T(8,128)}) %reduce-scatter.2.cloned.1.call-update) | async-done | bytes 131088 | tf_op jit(solution)/shard_map/reduce_scatter | solution.py:184
  608.8 2.3 fusion.26
  611.6 5.5 fusion.18
  622.0 75.0 %all-gather.12.cloned.1.call-done = f32[512,1024]{1,0:T(8,128)} async-done(((f32[32,1024]{1,0:T(8,128)}), f32[512,1024]{1,0:T(8,128)}) %all-gather.12.cloned.1.call-update) | async-done | bytes 2097168 | tf_op jit(solution)/shard_map/all_gather | solution.py:192
  696.9 2.4 reduce_sum.69
  (90 shorter events, 29.3 us)
Async XLA Ops:
  7.2 121.5 %all-gather.6.cloned.1.call-start = ((), (), s32[]{:S(2)}) async-start(), calls=%async_computation.1 | async-start | bytes 2162688 | tf_op jit(solution)/shard_map/all_gather | solution.py:148
  7.9 252.9 %all-gather.10.cloned.1.call-start = ((), (), s32[]{:S(2)}) async-start(), calls=%async_computation.3 | async-start | bytes 1081344 | tf_op jit(solution)/shard_map/all_gather | solution.py:149
  8.6 384.1 %all-gather.8.cloned.1.call-start = ((), (), s32[]{:S(2)}) async-start(), calls=%async_computation.2 | async-start | bytes 1081344 | tf_op jit(solution)/shard_map/all_gather | solution.py:147
  9.4 599.4 %reduce-scatter.2.cloned.1.call-start = ((), (), s32[]{:S(2)}) async-start(), calls=%async_computation.4 | async-start | bytes 4325376 | tf_op jit(solution)/shard_map/reduce_scatter | solution.py:184
  9.5 251.3 %copy-start.8 = (bf16[1,8,16,1024]{3,2,1,0:T(8,128)(2,1)S(1)}, bf16[1,8,16,1024]{3,2,1,0:T(8,128)(2,1)}, u32[]{:S(2)}) copy-start(bf16[1,8,16,1024]{3,2,1,0:T(8,128)(2,1)} %param.11) | copy-start | bytes 786436
  13.3 379.5 %copy-start.6 = (bf16[1,8,16,1024]{3,2,1,0:T(8,128)(2,1)}, bf16[1,8,16,1024]{3,2,1,0:T(8,128)(2,1)S(1)}, u32[]{:S(2)}) copy-start(bf16[1,8,16,1024]{3,2,1,0:T(8,128)(2,1)S(1)} %fusion.35) | copy-start | bytes 786436
  130.7 131.9 %collective-permute-start = (bf16[1,6,16,1024]{3,2,1,0:T(8,128)(2,1)S(1)}, bf16[1,6,16,1024]{3,2,1,0:T(8,128)(2,1)S(1)}, u32[]{:S(2)}, u32[]{:S(2)}) collective-permute-start(bf16[1,6,16,1024]{3,2,1,0:T(8,128)(2,1)S(1)} %get-tuple-element.11), channel_id=1, source_target_pairs={{0,16},{16,32},{32,48},{48,64},{64,80},{80,96},{96,112},{112,128},... | collective-permute-start | bytes 589832 | tf_op jit(solution)/shard_map/ppermute | solution.py:24
  132.9 129.8 %collective-permute-start.1 = (bf16[1,6,16,1024]{3,2,1,0:T(8,128)(2,1)S(1)}, bf16[1,6,16,1024]{3,2,1,0:T(8,128)(2,1)S(1)}, u32[]{:S(2)}, u32[]{:S(2)}) collective-permute-start(bf16[1,6,16,1024]{3,2,1,0:T(8,128)(2,1)S(1)} %get-tuple-element.12), channel_id=1, source_target_pairs={{16,0},{32,16},{48,32},{64,48},{80,64},{96,80},{112,96},{128,112},... | collective-permute-start | bytes 589832 | tf_op jit(solution)/shard_map/ppermute | solution.py:27
  262.9 131.6 %collective-permute-start.2 = (bf16[1,20,6,1024]{3,2,1,0:T(8,128)(2,1)S(1)}, bf16[1,20,6,1024]{3,2,1,0:T(8,128)(2,1)S(1)}, u32[]{:S(2)}, u32[]{:S(2)}) collective-permute-start(bf16[1,20,6,1024]{3,2,1,0:T(8,128)(2,1)S(1)} %get-tuple-element.9), channel_id=1, source_target_pairs={{0,1},{1,2},{2,3},{3,4},{4,5},{5,6},{6,7},{7,8},{8,9},{9,10},{10,1... | collective-permute-start | bytes 737288 | tf_op jit(solution)/shard_map/ppermute | solution.py:24
  288.8 105.7 %collective-permute-start.3 = (bf16[1,20,6,1024]{3,2,1,0:T(8,128)(2,1)S(1)}, bf16[1,20,6,1024]{3,2,1,0:T(8,128)(2,1)S(1)}, u32[]{:S(2)}, u32[]{:S(2)}) collective-permute-start(bf16[1,20,6,1024]{3,2,1,0:T(8,128)(2,1)S(1)} %get-tuple-element.10), channel_id=1, source_target_pairs={{1,0},{2,1},{3,2},{4,3},{5,4},{6,5},{7,6},{8,7},{9,8},{10,9},{11,1... | collective-permute-start | bytes 737288 | tf_op jit(solution)/shard_map/ppermute | solution.py:27
  394.5 6.0 copy-start.13
  395.8 4.7 copy-start.11
  396.1 4.4 copy-start.4
  421.6 37.2 %collective-permute-start.4 = (f32[1,20,6,1024]{3,0,2,1:T(1,128)S(1)}, f32[1,20,6,1024]{3,0,2,1:T(1,128)S(1)}, u32[]{:S(2)}, u32[]{:S(2)}) collective-permute-start(f32[1,20,6,1024]{3,0,2,1:T(1,128)S(1)} %get-tuple-element.3), channel_id=1, source_target_pairs={{0,1},{1,2},{2,3},{3,4},{4,5},{5,6},{6,7},{7,8},{8,9},{9,10},{10,1... | collective-permute-start | bytes 1474568 | tf_op jit(solution)/shard_map/ppermute | solution.py:16
  447.5 11.7 %collective-permute-start.5 = (f32[1,20,6,1024]{3,0,2,1:T(1,128)S(1)}, f32[1,20,6,1024]{3,0,2,1:T(1,128)S(1)}, u32[]{:S(2)}, u32[]{:S(2)}) collective-permute-start(f32[1,20,6,1024]{3,0,2,1:T(1,128)S(1)} %get-tuple-element.4), channel_id=1, source_target_pairs={{1,0},{2,1},{3,2},{4,3},{5,4},{6,5},{7,6},{8,7},{9,8},{10,9},{11,1... | collective-permute-start | bytes 1474568 | tf_op jit(solution)/shard_map/ppermute | solution.py:16
  460.7 16.2 %copy-start.7 = (bf16[1,8,16,1024]{3,2,1,0:T(8,128)(2,1)S(1)}, bf16[1,8,16,1024]{3,2,1,0:T(8,128)(2,1)}, u32[]{:S(2)}) copy-start(bf16[1,8,16,1024]{3,2,1,0:T(8,128)(2,1)} %copy-done.6) | copy-start | bytes 786436
  461.2 14.2 %collective-permute-start.6 = (f32[1,6,16,1024]{3,0,2,1:T(1,128)S(1)}, f32[1,6,16,1024]{3,0,2,1:T(1,128)S(1)}, u32[]{:S(2)}, u32[]{:S(2)}) collective-permute-start(f32[1,6,16,1024]{3,0,2,1:T(1,128)S(1)} %get-tuple-element.5), channel_id=1, source_target_pairs={{0,16},{16,32},{32,48},{48,64},{64,80},{80,96},{96,112},{112,128},... | collective-permute-start | bytes 1179656 | tf_op jit(solution)/shard_map/ppermute | solution.py:16
  462.5 12.9 %collective-permute-start.7 = (f32[1,6,16,1024]{3,0,2,1:T(1,128)S(1)}, f32[1,6,16,1024]{3,0,2,1:T(1,128)S(1)}, u32[]{:S(2)}, u32[]{:S(2)}) collective-permute-start(f32[1,6,16,1024]{3,0,2,1:T(1,128)S(1)} %get-tuple-element.6), channel_id=1, source_target_pairs={{16,0},{32,16},{48,32},{64,48},{80,64},{96,80},{112,96},{128,112},... | collective-permute-start | bytes 1179656 | tf_op jit(solution)/shard_map/ppermute | solution.py:16
  479.5 129.3 %copy-start.5 = (bf16[1,560,512]{1,2,0:T(8,128)(2,1)S(1)}, bf16[1,560,512]{1,2,0:T(8,128)(2,1)}, u32[]{:S(2)}) copy-start(bf16[1,560,512]{1,2,0:T(8,128)(2,1)} %copy-done.4) | copy-start | bytes 1720324
  479.5 129.3 %copy-start.14 = (bf16[128,512]{0,1:T(8,128)(2,1)S(1)}, bf16[128,512]{0,1:T(8,128)(2,1)}, u32[]{:S(2)}) copy-start(bf16[128,512]{0,1:T(8,128)(2,1)} %copy-done.13) | copy-start | bytes 393220
  479.6 217.4 %all-gather.12.cloned.1.call-start = ((), (), s32[]{:S(2)}) async-start(), calls=%async_computation.5 | async-start | bytes 2228224 | tf_op jit(solution)/shard_map/all_gather | solution.py:192
  611.6 5.6 copy-start
  611.6 5.6 copy-start.3
  611.6 6.6 copy-start.1
  (5 other events, 12.1 us)
Sparse Core Ops, SparseCore 0:
  10.1 118.4 all-gather.5
  130.7 130.0 all-gather.9
  262.9 129.8 all-gather.7
  479.7 129.0 reduce-scatter.1
  611.9 84.9 all-gather.11
